TPU v7x, 32 devices: a whole 2x2x4 slice. The times are simulated.
32 devices in a mesh: groups: 2 (over y), ctx: 4 (over z), head: 4 (over x, core).
Axes of the slice: x: 2, y: 2, z: 4, core: 2. Of those that a mesh axis runs over, the one named last changes fastest.
Arguments:
- queries: bfloat16 [8192, 512], P(('groups', 'ctx', 'head')), parts along dimension 0, may hold values from -8 to 8, as said below
- keys: bfloat16 [8192, 512], P(('groups', 'ctx', 'head')), parts along dimension 0, may hold values from -8 to 8
- values: bfloat16 [8192, 4096], P(('groups', 'ctx', 'head')), parts along dimension 0, may hold values from -6 to 6
- gain: float32 [4096], P('head'), may hold values from 0.5 to 1.5
Outputs:
- mixed: bfloat16 [8192, 4096], P(('groups', 'ctx', 'head')), parts along dimension 0
There are 2 independent parts, one for each index of `groups`. A program takes and returns all parts, laid end to end along the dimension named above; an argument that names none is the same for every part. Nothing has to cross between parts.
Inputs may be any that keep to these rules, and one draw needn't show every extreme that they name: `queries`: query entries lie in the stated range.
All inputs are finite; a program needn't handle non-finite values.
Results may differ from a plain program's by a relative error of at most 0.0054.
Values may be sent and summed in bfloat16 or wider, within the bound.
No kernel may reach another device: no remote copies, remote signals or barrier semaphores. Data moves between devices by JAX's collectives and lax.ppermute only.
A program may use at most 128 MiB of HBM per device.

v0:
```python
import math
import jax
import numpy as np
import jax.numpy as jnp
from jax import lax
from jax.sharding import PartitionSpec as P

HEADS = 32
KD = 16
VD = 128
WINDOW = 64
outer_scale = 1.0 / (4.0 * math.sqrt(2.0))
epsilon = 1e-06


def shifted(shard, axis, by):
    peers = lax.axis_size(axis)
    pairs = [(i, i + by) for i in range(peers) if 0 <= i + by < peers]
    return lax.ppermute(shard, axis, pairs)


def unique_features(vector, doubled):
    rows, cols = np.triu_indices(KD)
    pick_rows = jnp.asarray(np.eye(KD)[:, rows], jnp.bfloat16)
    pick_cols = jnp.asarray(np.eye(KD)[:, cols], jnp.bfloat16)
    first = jnp.einsum("...d,df->...f", vector, pick_rows, preferred_element_type=jnp.float32)
    second = jnp.einsum("...d,df->...f", vector, pick_cols, preferred_element_type=jnp.float32)
    prod = (first * second * outer_scale).astype(jnp.bfloat16)
    if doubled:
        prod = prod * jnp.asarray(np.where(rows == cols, 1.0, 2.0), jnp.bfloat16)
    lead = vector.shape[:-1]
    unit = jnp.ones(lead + (1,), jnp.bfloat16)
    half = (vector.astype(jnp.float32) * 0.5).astype(jnp.bfloat16)
    return jnp.concatenate([unit, half, prod], axis=-1)


def attend(query_head, key_head, value_head, gains, first_span):
    span_rows = query_head.shape[0]
    heads_here = query_head.shape[1]
    block_rows = min(512, span_rows)
    block_count = span_rows // block_rows
    key_feat = unique_features(key_head, False)
    feat = key_feat.shape[-1]
    block_states = jnp.einsum(
        "nrhf,nrhv->nhfv",
        key_feat.reshape(block_count, block_rows, heads_here, feat),
        value_head.reshape(block_count, block_rows, heads_here, VD),
        preferred_element_type=jnp.float32,
    )
    span_state = jnp.sum(block_states, axis=0)
    everything = lax.all_gather(span_state, "ctx")
    peers = everything.shape[0]
    here = lax.axis_index("ctx")
    entering = jnp.sum(
        jnp.where(
            (jnp.arange(peers) < here)[:, None, None, None], everything, jnp.zeros_like(everything)
        ),
        axis=0,
    )
    before = jnp.concatenate(
        [jnp.zeros_like(block_states[:1]), jnp.cumsum(block_states[:-1], axis=0)], axis=0
    )
    states = (before + entering[None]).astype(jnp.bfloat16)
    query_blocks = query_head.reshape(block_count, block_rows, heads_here, KD)
    key_blocks = key_head.reshape(block_count, block_rows, heads_here, KD)
    value_blocks = value_head.reshape(block_count, block_rows, heads_here, VD)
    scores = (
        jnp.einsum("nrhd,nshd->nhrs", query_blocks, key_blocks, preferred_element_type=jnp.float32)
        * 0.25
    )
    row_pos = jnp.arange(block_rows)[:, None]
    col_pos = jnp.arange(block_rows)[None, :]
    kernel = jnp.where(col_pos <= row_pos, 1.0 + scores + 0.5 * scores * scores, 0.0).astype(
        jnp.bfloat16
    )
    intra = jnp.einsum("nhrs,nshv->nrhv", kernel, value_blocks, preferred_element_type=jnp.float32)
    query_feat = unique_features(query_blocks, True)
    inter = jnp.einsum("nrhf,nhfv->nrhv", query_feat, states, preferred_element_type=jnp.float32)
    linear = (intra + inter).reshape(span_rows, heads_here, VD)
    tails = shifted(jnp.concatenate([key_head, value_head], axis=2)[span_rows - WINDOW :], "ctx", 1)
    tail_keys = tails[:, :, :KD]
    tail_values = tails[:, :, KD:]
    chunks = span_rows // WINDOW
    key_prev = jnp.concatenate([tail_keys, key_head[: span_rows - WINDOW]], axis=0)
    value_prev = jnp.concatenate([tail_values, value_head[: span_rows - WINDOW]], axis=0)
    key_win = jnp.concatenate(
        [
            key_prev.reshape(chunks, WINDOW, heads_here, KD),
            key_head.reshape(chunks, WINDOW, heads_here, KD),
        ],
        axis=1,
    )
    value_win = jnp.concatenate(
        [
            value_prev.reshape(chunks, WINDOW, heads_here, VD),
            value_head.reshape(chunks, WINDOW, heads_here, VD),
        ],
        axis=1,
    )
    query_chunks = query_head.reshape(chunks, WINDOW, heads_here, KD)
    window_scores = (
        jnp.einsum("crhd,cphd->chrp", query_chunks, key_win, preferred_element_type=jnp.float32)
        * 0.25
    )
    r_pos = jnp.arange(WINDOW)[:, None]
    p_pos = jnp.arange(2 * WINDOW)[None, :]
    chunk_pos = jnp.arange(chunks)[:, None, None, None]
    valid = (p_pos > r_pos) & (p_pos <= r_pos + WINDOW)
    valid = valid[None, None] & ((chunk_pos > 0) | (p_pos >= WINDOW) | jnp.logical_not(first_span))
    masked = jnp.where(valid, window_scores, -jnp.inf)
    highest_score = jnp.max(masked, axis=3, keepdims=True)
    expo = jnp.where(valid, jnp.exp(window_scores - highest_score), 0.0)
    weights = (expo / jnp.sum(expo, axis=3, keepdims=True)).astype(jnp.bfloat16)
    window = jnp.einsum(
        "chrp,cphv->crhv", weights, value_win, preferred_element_type=jnp.float32
    ).reshape(span_rows, heads_here, VD)
    scale = lax.rsqrt(jnp.mean(linear * linear, axis=2, keepdims=True) + epsilon)
    return (linear * scale * gains + window).astype(jnp.bfloat16)


def per_device(queries, keys, values, gain):
    local_tokens = queries.shape[0]
    peers = lax.axis_size("head")
    heads_here = HEADS // peers
    groups = 2 if heads_here % 2 == 0 else 1
    group_heads = heads_here // groups
    query_tok = queries.reshape(local_tokens, peers, groups, group_heads, KD)
    key_tok = keys.reshape(local_tokens, peers, groups, group_heads, KD)
    value_tok = values.reshape(local_tokens, peers, groups, group_heads, VD)
    gains = gain.reshape(groups, group_heads, VD)
    first_span = lax.axis_index("ctx") == 0
    span_rows = local_tokens * peers

    def gathered(tok, g, width):
        moved = lax.all_to_all(tok[:, :, g], "head", split_axis=1, concat_axis=0, tiled=True)
        return moved.reshape(span_rows, group_heads, width)

    outs = []
    for g in range(groups):
        mixed = attend(
            gathered(query_tok, g, KD),
            gathered(key_tok, g, KD),
            gathered(value_tok, g, VD),
            gains[g],
            first_span,
        )
        back = lax.all_to_all(mixed, "head", split_axis=0, concat_axis=1, tiled=True)
        outs.append(back.reshape(local_tokens, peers, group_heads, VD))
    tokens_back = jnp.stack(outs, axis=2)
    return tokens_back.reshape(local_tokens, HEADS * VD)


def solution(mesh):
    placed = (
        P(("groups", "ctx", "head"), None),
        P(("groups", "ctx", "head"), None),
        P(("groups", "ctx", "head"), None),
        P("head"),
    )
    return jax.shard_map(
        per_device,
        mesh=mesh,
        in_specs=placed,
        out_specs=P(("groups", "ctx", "head"), None),
        check_vma=False,
    )
```

profile of v0, /device:TPU:0, one launch (start us, length us, event | category | flops | bytes accessed | tf_op | source)
XLA Modules:
  0.0 217.1 jit_solution(292104657550504875)
XLA Ops:
  8.4 4.2 %all-to-all-start.5 = ((bf16[256,4,4,16]{0,3,2,1:T(8,128)(2,1)}), bf16[256,4,4,16]{0,3,2,1:T(8,128)(2,1)S(1)}, u32[]{:S(2)}, u32[]{:S(2)}) async-start(bf16[256,4,4,16]{0,3,2,1:T(8,128)(2,1)} %get-tuple-element.12), calls=%async_computation.5 | async-start | bytes 262144 | tf_op jit(solution)/shard_map/all_to_all | solution.py:135
  12.6 3.3 %copy.132 = bf16[256,4096]{0,1:T(8,128)(2,1)S(1)} copy(bf16[256,4096]{1,0:T(8,128)(2,1)} %param.16) | data formatting | bytes 4194304 | tf_op args[2]
  20.0 3.3 %all-to-all-start.1 = ((bf16[256,4,4,16]{0,3,2,1:T(8,128)(2,1)}), bf16[256,4,4,16]{0,3,2,1:T(8,128)(2,1)S(1)}, u32[]{:S(2)}, u32[]{:S(2)}) async-start(bf16[256,4,4,16]{0,3,2,1:T(8,128)(2,1)} %get-tuple-element.11), calls=%async_computation.1 | async-start | bytes 262144 | tf_op jit(solution)/shard_map/all_to_all | solution.py:135
  23.5 4.4 %all-to-all-done.1 = bf16[256,4,4,16]{0,3,2,1:T(8,128)(2,1)S(1)} async-done(((bf16[256,4,4,16]{0,3,2,1:T(8,128)(2,1)}), bf16[256,4,4,16]{0,3,2,1:T(8,128)(2,1)S(1)}, u32[]{:S(2)}, u32[]{:S(2)}) %all-to-all-start.1) | async-done | bytes 131104 | tf_op jit(solution)/shard_map/all_to_all | solution.py:135
  27.9 3.3 %all-to-all-start.4 = ((bf16[256,4,4,16]{0,3,2,1:T(8,128)(2,1)}), bf16[256,4,4,16]{0,3,2,1:T(8,128)(2,1)S(1)}, u32[]{:S(2)}, u32[]{:S(2)}) async-start(bf16[256,4,4,16]{0,3,2,1:T(8,128)(2,1)} %get-tuple-element.10), calls=%async_computation.4 | async-start | bytes 262144 | tf_op jit(solution)/shard_map/all_to_all | solution.py:135
  35.9 3.3 %all-to-all-start = ((bf16[256,4,4,16]{0,3,2,1:T(8,128)(2,1)}), bf16[256,4,4,16]{0,3,2,1:T(8,128)(2,1)S(1)}, u32[]{:S(2)}, u32[]{:S(2)}) async-start(bf16[256,4,4,16]{0,3,2,1:T(8,128)(2,1)} %get-tuple-element.9), calls=%async_computation | async-start | bytes 262144 | tf_op jit(solution)/shard_map/all_to_all | solution.py:135
  40.1 3.7 %all-to-all-done = bf16[256,4,4,16]{0,3,2,1:T(8,128)(2,1)S(1)} async-done(((bf16[256,4,4,16]{0,3,2,1:T(8,128)(2,1)}), bf16[256,4,4,16]{0,3,2,1:T(8,128)(2,1)S(1)}, u32[]{:S(2)}, u32[]{:S(2)}) %all-to-all-start) | async-done | bytes 131104 | tf_op jit(solution)/shard_map/all_to_all | solution.py:135
  43.8 3.5 %all-to-all-start.2 = ((bf16[256,4,4,128]{0,3,2,1:T(8,128)(2,1)}), bf16[256,4,4,128]{0,3,2,1:T(8,128)(2,1)S(1)}, u32[]{:S(2)}, u32[]{:S(2)}) async-start(bf16[256,4,4,128]{0,3,2,1:T(8,128)(2,1)} %get-tuple-element.7), calls=%async_computation.2 | async-start | bytes 2097152 | tf_op jit(solution)/shard_map/all_to_all | solution.py:135
  52.3 9.4 %all-to-all-done.2 = bf16[256,4,4,128]{0,3,2,1:T(8,128)(2,1)S(1)} async-done(((bf16[256,4,4,128]{0,3,2,1:T(8,128)(2,1)}), bf16[256,4,4,128]{0,3,2,1:T(8,128)(2,1)S(1)}, u32[]{:S(2)}, u32[]{:S(2)}) %all-to-all-start.2) | async-done | bytes 1048608 | tf_op jit(solution)/shard_map/all_to_all | solution.py:135
  61.7 3.5 %all-to-all-start.6 = ((bf16[256,4,4,128]{0,3,2,1:T(8,128)(2,1)}), bf16[256,4,4,128]{0,3,2,1:T(8,128)(2,1)S(1)}, u32[]{:S(2)}, u32[]{:S(2)}) async-start(bf16[256,4,4,128]{0,3,2,1:T(8,128)(2,1)} %get-tuple-element.8), calls=%async_computation.6 | async-start | bytes 2097152 | tf_op jit(solution)/shard_map/all_to_all | solution.py:135
  65.3 3.7 %pad_maximum_fusion.3 = (bf16[1024,4,153]{0,2,1:T(8,128)(2,1)}, bf16[1024,4,153]{0,2,1:T(8,128)(2,1)S(1)}) fusion(bf16[1024,4,136]{0,2,1:T(8,128)(2,1)} %fusion.32, bf16[1024,4,16]{0,2,1:T(8,128)(2,1)} %multiply_convert_fusion.7, bf16[153]{0:T(256)(128)(2,1)S(1)} %pad.33.clone, bf16[1024,4,136]{0,2,1:T(8,128)(2,1)} %fusion.35, ...), kind=kLoop, calls=%fused_computation.55 | loop fusion | flops 6893568 | bytes 4997426 | tf_op jit(solution)/shard_map/concatenate | solution.py:34
  74.6 3.7 %fusion.110 = (f32[4,153,128]{2,1,0:T(8,128)}, f32[2,4,153,128]{3,2,1,0:T(8,128)}) fusion(bf16[2,512,4,128]{3,1,0,2:T(8,128)(2,1)} %bitcast.198, bf16[2,512,4,153]{1,0,3,2:T(2,128)(2,1)} %reshape.229), kind=kOutput, calls=%fused_computation.158 | convolution fusion | flops 160510464 | bytes 3241984 | tf_op jit(solution)/shard_map/nrhf,nrhv->nhfv/dot_general | solution.py:44
  102.0 4.7 %collective-permute-start.1 = (bf16[64,4,144]{0,2,1:T(8,128)(2,1)}, bf16[64,4,144]{0,2,1:T(8,128)(2,1)}, u32[]{:S(2)}, u32[]{:S(2)}) collective-permute-start(bf16[64,4,144]{0,2,1:T(8,128)(2,1)} %pad_maximum_fusion.7), channel_id=1, source_target_pairs={{0,4},{4,8},{8,12},{1,5},{5,9},{9,13},{2,6},{6,10},{10,14},{3,7},{... | collective-permute-start | bytes 221192 | tf_op jit(solution)/shard_map/ppermute | solution.py:19
  108.2 3.8 %collective-permute-start = (bf16[64,4,144]{0,2,1:T(8,128)(2,1)}, bf16[64,4,144]{0,2,1:T(8,128)(2,1)}, u32[]{:S(2)}, u32[]{:S(2)}) collective-permute-start(bf16[64,4,144]{0,2,1:T(8,128)(2,1)} %pad_maximum_fusion.8), channel_id=1, source_target_pairs={{0,4},{4,8},{8,12},{1,5},{5,9},{9,13},{2,6},{6,10},{10,14},{3,7},{... | collective-permute-start | bytes 221192 | tf_op jit(solution)/shard_map/ppermute | solution.py:19
  112.1 5.5 %fusion.2 = f32[2,4,512,128]{3,2,1,0:T(8,128)} fusion(pred[512,512]{1,0:T(8,128)(4,1)} %iota_compare_fusion, bf16[2,512,4,128]{3,1,0,2:T(8,128)(2,1)} %bitcast.199, bf16[2,512,4,16]{1,0,3,2:T(2,128)(2,1)} %reshape_reshape.39, bf16[2,512,4,16]{1,0,3,2:T(2,128)(2,1)S(1)} %copy-done.9), kind=kOutput, calls=%fused_computation.4 | convolution fusion | flops 618659840 | bytes 3670016 | tf_op jit(solution)/shard_map/nhrs,nshv->nrhv/dot_general | solution.py:76
  117.6 5.6 %fusion.3 = f32[2,4,512,128]{3,2,1,0:T(8,128)} fusion(pred[512,512]{1,0:T(8,128)(4,1)} %iota_compare_fusion, bf16[2,512,4,128]{3,1,0,2:T(8,128)(2,1)} %bitcast.201, bf16[2,512,4,16]{1,0,3,2:T(2,128)(2,1)} %reshape_reshape.45, bf16[2,512,4,16]{1,0,3,2:T(2,128)(2,1)S(1)} %copy-done.7), kind=kOutput, calls=%fused_computation.5 | convolution fusion | flops 618659840 | bytes 3670016 | tf_op jit(solution)/shard_map/nhrs,nshv->nrhv/dot_general | solution.py:76
  145.9 3.3 %fusion.112 = (f32[16,4,64]{2,1,0:T(4,128)S(1)}, f32[16,4,64,128]{3,2,1,0:T(8,128)S(1)}) fusion(f32[16,4,128,64]{2,3,1,0:T(8,128)S(1)} %fusion.66, pred[16,64,128]{2,1,0:T(8,128)(4,1)S(1)} %copy-done.27), kind=kOutput, calls=%fused_computation.160 | output fusion | flops 3145855 | bytes 4341760 | tf_op jit(solution)/shard_map/sub | solution.py:112
  152.2 7.0 %all-gather.7.cloned.1.call-done = f32[16,153,128]{2,1,0:T(8,128)} async-done(((f32[4,153,128]{2,1,0:T(8,128)}), f32[16,153,128]{2,1,0:T(8,128)}) %all-gather.7.cloned.1.call-update) | async-done | bytes 1253392 | tf_op jit(solution)/shard_map/all_gather | solution.py:51
  167.6 3.5 %all-to-all-start.7 = ((bf16[1024,4,128]{2,1,0:T(4,128)(2,1)}), bf16[1024,4,128]{2,1,0:T(4,128)(2,1)S(1)}, u32[]{:S(2)}, u32[]{:S(2)}) async-start(bf16[1024,4,128]{2,1,0:T(4,128)(2,1)} %copy.181), calls=%async_computation.7 | async-start | bytes 2097152 | tf_op jit(solution)/shard_map/all_to_all | solution.py:147
  171.2 3.0 %multiply_reduce_fusion.1 = (f32[2,512,4]{1,2,0:T(4,128)S(1)}, f32[2,512,4,128]{3,1,2,0:T(8,128)S(1)}) fusion(bf16[2,512,4,136]{1,3,2,0:T(8,128)(2,1)S(1)} %copy-done.3, bf16[2,512,4,16]{1,3,2,0:T(8,128)(2,1)S(1)} %copy-done.22, bf16[153]{0:T(256)(128)(2,1)S(1)} %pad.33.clone, f32[1,4,153,128]{3,2,1,0:T(8,128)S(1)} %copy-done.13, ...), kind=kOutput, calls=%fused_computation.42 | convolution fusion | flops 166074368 | bytes 6082866 | tf_op jit(solution)/shard_map/nrhf,nhfv->nrhv/dot_general | solution.py:78
  178.5 7.0 %all-to-all-done.7 = bf16[1024,4,128]{2,1,0:T(4,128)(2,1)S(1)} async-done(((bf16[1024,4,128]{2,1,0:T(4,128)(2,1)}), bf16[1024,4,128]{2,1,0:T(4,128)(2,1)S(1)}, u32[]{:S(2)}, u32[]{:S(2)}) %all-to-all-start.7) | async-done | bytes 1048608 | tf_op jit(solution)/shard_map/all_to_all | solution.py:147
  185.5 3.5 %all-to-all-start.3 = ((bf16[1024,4,128]{2,1,0:T(4,128)(2,1)}), bf16[1024,4,128]{2,1,0:T(4,128)(2,1)S(1)}, u32[]{:S(2)}, u32[]{:S(2)}) async-start(bf16[1024,4,128]{2,1,0:T(4,128)(2,1)} %copy.154), calls=%async_computation.3 | async-start | bytes 2097152 | tf_op jit(solution)/shard_map/all_to_all | solution.py:147
  189.2 14.3 %all-to-all-done.3 = bf16[1024,4,128]{2,1,0:T(4,128)(2,1)S(1)} async-done(((bf16[1024,4,128]{2,1,0:T(4,128)(2,1)}), bf16[1024,4,128]{2,1,0:T(4,128)(2,1)S(1)}, u32[]{:S(2)}, u32[]{:S(2)}) %all-to-all-start.3) | async-done | bytes 1048608 | tf_op jit(solution)/shard_map/all_to_all | solution.py:147
  206.2 4.1 %copy.184 = bf16[256,4096]{1,0:T(8,128)(2,1)} copy(bf16[256,4096]{0,1:T(8,128)(2,1)} %bitcast.191) | data formatting | bytes 4194304 | tf_op jit(solution)/shard_map/reshape | solution.py:150
  (169 shorter events, 88.3 us)
Async XLA Ops:
  8.4 11.6 %all-to-all-start.5 = ((bf16[256,4,4,16]{0,3,2,1:T(8,128)(2,1)}), bf16[256,4,4,16]{0,3,2,1:T(8,128)(2,1)S(1)}, u32[]{:S(2)}, u32[]{:S(2)}) async-start(bf16[256,4,4,16]{0,3,2,1:T(8,128)(2,1)} %get-tuple-element.12), calls=%async_computation.5 | async-start | bytes 262144 | tf_op jit(solution)/shard_map/all_to_all | solution.py:135
  17.4 14.1 %copy-start.31 = (bf16[16,136,1]{1,0,2:T(8,128)(2,1)S(1)}, bf16[16,136,1]{1,0,2:T(8,128)(2,1)}, u32[]{:S(2)}) copy-start(bf16[16,136,1]{1,0,2:T(8,128)(2,1)} %constant.58) | copy-start | bytes 13060
  20.0 8.0 %all-to-all-start.1 = ((bf16[256,4,4,16]{0,3,2,1:T(8,128)(2,1)}), bf16[256,4,4,16]{0,3,2,1:T(8,128)(2,1)S(1)}, u32[]{:S(2)}, u32[]{:S(2)}) async-start(bf16[256,4,4,16]{0,3,2,1:T(8,128)(2,1)} %get-tuple-element.11), calls=%async_computation.1 | async-start | bytes 262144 | tf_op jit(solution)/shard_map/all_to_all | solution.py:135
  23.4 7.8 %copy-start.10 = (bf16[4,256,1,4,16]{1,0,4,3,2:T(4,128)(2,1)}, bf16[4,256,1,4,16]{1,0,4,3,2:T(4,128)(2,1)S(1)}, u32[]{:S(2)}) copy-start(bf16[4,256,1,4,16]{1,0,4,3,2:T(4,128)(2,1)S(1)} %copy.157) | copy-start | bytes 393220
  23.5 25.0 %copy-start.1 = (bf16[1024,4,16]{0,2,1:T(8,128)(2,1)}, bf16[1024,4,16]{0,2,1:T(8,128)(2,1)S(1)}, u32[]{:S(2)}) copy-start(bf16[1024,4,16]{0,2,1:T(8,128)(2,1)S(1)} %reshape.235) | copy-start | bytes 393220
  27.9 7.9 %all-to-all-start.4 = ((bf16[256,4,4,16]{0,3,2,1:T(8,128)(2,1)}), bf16[256,4,4,16]{0,3,2,1:T(8,128)(2,1)S(1)}, u32[]{:S(2)}, u32[]{:S(2)}) async-start(bf16[256,4,4,16]{0,3,2,1:T(8,128)(2,1)} %get-tuple-element.10), calls=%async_computation.4 | async-start | bytes 262144 | tf_op jit(solution)/shard_map/all_to_all | solution.py:135
  35.4 12.1 %copy-start.29 = (bf16[16,136,1,1]{1,0,3,2:T(8,128)(2,1)S(1)}, bf16[16,136,1,1]{1,0,3,2:T(8,128)(2,1)}, u32[]{:S(2)}) copy-start(bf16[16,136,1,1]{1,0,3,2:T(8,128)(2,1)} %constant.60) | copy-start | bytes 13060
  35.9 7.9 %all-to-all-start = ((bf16[256,4,4,16]{0,3,2,1:T(8,128)(2,1)}), bf16[256,4,4,16]{0,3,2,1:T(8,128)(2,1)S(1)}, u32[]{:S(2)}, u32[]{:S(2)}) async-start(bf16[256,4,4,16]{0,3,2,1:T(8,128)(2,1)} %get-tuple-element.9), calls=%async_computation | async-start | bytes 262144 | tf_op jit(solution)/shard_map/all_to_all | solution.py:135
  40.1 9.1 %copy-start.6 = (bf16[2,512,4,16]{1,0,3,2:T(2,128)(2,1)}, bf16[2,512,4,16]{1,0,3,2:T(2,128)(2,1)S(1)}, u32[]{:S(2)}) copy-start(bf16[2,512,4,16]{1,0,3,2:T(2,128)(2,1)S(1)} %reshape_reshape.44) | copy-start | bytes 393220
  43.8 18.0 %all-to-all-start.2 = ((bf16[256,4,4,128]{0,3,2,1:T(8,128)(2,1)}), bf16[256,4,4,128]{0,3,2,1:T(8,128)(2,1)S(1)}, u32[]{:S(2)}, u32[]{:S(2)}) async-start(bf16[256,4,4,128]{0,3,2,1:T(8,128)(2,1)} %get-tuple-element.7), calls=%async_computation.2 | async-start | bytes 2097152 | tf_op jit(solution)/shard_map/all_to_all | solution.py:135
  61.7 33.8 %all-to-all-start.6 = ((bf16[256,4,4,128]{0,3,2,1:T(8,128)(2,1)}), bf16[256,4,4,128]{0,3,2,1:T(8,128)(2,1)S(1)}, u32[]{:S(2)}, u32[]{:S(2)}) async-start(bf16[256,4,4,128]{0,3,2,1:T(8,128)(2,1)} %get-tuple-element.8), calls=%async_computation.6 | async-start | bytes 2097152 | tf_op jit(solution)/shard_map/all_to_all | solution.py:135
  65.3 86.9 %all-gather.5.cloned.1.call-start = ((), (), s32[]{:S(2)}) async-start(), calls=%async_computation.8 | async-start | bytes 1638400 | tf_op jit(solution)/shard_map/all_gather | solution.py:51
  78.3 80.9 %all-gather.7.cloned.1.call-start = ((), (), s32[]{:S(2)}) async-start(), calls=%async_computation.9 | async-start | bytes 1638400 | tf_op jit(solution)/shard_map/all_gather | solution.py:51
  101.3 10.8 %copy-start.9 = (bf16[2,512,4,16]{1,0,3,2:T(2,128)(2,1)S(1)}, bf16[2,512,4,16]{1,0,3,2:T(2,128)(2,1)}, u32[]{:S(2)}) copy-start(bf16[2,512,4,16]{1,0,3,2:T(2,128)(2,1)} %copy-done.8) | copy-start | bytes 393220
  102.0 25.3 %collective-permute-start.1 = (bf16[64,4,144]{0,2,1:T(8,128)(2,1)}, bf16[64,4,144]{0,2,1:T(8,128)(2,1)}, u32[]{:S(2)}, u32[]{:S(2)}) collective-permute-start(bf16[64,4,144]{0,2,1:T(8,128)(2,1)} %pad_maximum_fusion.7), channel_id=1, source_target_pairs={{0,4},{4,8},{8,12},{1,5},{5,9},{9,13},{2,6},{6,10},{10,14},{3,7},{... | collective-permute-start | bytes 221192 | tf_op jit(solution)/shard_map/ppermute | solution.py:19
  108.2 9.3 %copy-start.7 = (bf16[2,512,4,16]{1,0,3,2:T(2,128)(2,1)S(1)}, bf16[2,512,4,16]{1,0,3,2:T(2,128)(2,1)}, u32[]{:S(2)}) copy-start(bf16[2,512,4,16]{1,0,3,2:T(2,128)(2,1)} %copy-done.6) | copy-start | bytes 393220
  108.2 28.5 %collective-permute-start = (bf16[64,4,144]{0,2,1:T(8,128)(2,1)}, bf16[64,4,144]{0,2,1:T(8,128)(2,1)}, u32[]{:S(2)}, u32[]{:S(2)}) collective-permute-start(bf16[64,4,144]{0,2,1:T(8,128)(2,1)} %pad_maximum_fusion.8), channel_id=1, source_target_pairs={{0,4},{4,8},{8,12},{1,5},{5,9},{9,13},{2,6},{6,10},{10,14},{3,7},{... | collective-permute-start | bytes 221192 | tf_op jit(solution)/shard_map/ppermute | solution.py:19
  117.6 5.6 %copy-start.17 = (bf16[4,256,1,4,128]{4,1,0,3,2:T(8,128)(2,1)S(1)}, bf16[4,256,1,4,128]{4,1,0,3,2:T(8,128)(2,1)}, u32[]{:S(2)}) copy-start(bf16[4,256,1,4,128]{4,1,0,3,2:T(8,128)(2,1)} %copy.160) | copy-start | bytes 3145732
  150.6 11.5 %copy-start.23 = (bf16[2,512,4,16]{1,3,2,0:T(8,128)(2,1)S(1)}, bf16[2,512,4,16]{1,3,2,0:T(8,128)(2,1)}, u32[]{:S(2)}) copy-start(bf16[2,512,4,16]{1,3,2,0:T(8,128)(2,1)} %multiply_convert_fusion.4) | copy-start | bytes 393220
  152.2 9.9 %copy-start.4 = (bf16[2,512,4,136]{1,3,2,0:T(8,128)(2,1)S(1)}, bf16[2,512,4,136]{1,3,2,0:T(8,128)(2,1)}, u32[]{:S(2)}) copy-start(bf16[2,512,4,136]{1,3,2,0:T(8,128)(2,1)} %fusion.37) | copy-start | bytes 3342340
  165.8 5.4 %copy-start.3 = (bf16[2,512,4,136]{1,3,2,0:T(8,128)(2,1)S(1)}, bf16[2,512,4,136]{1,3,2,0:T(8,128)(2,1)}, u32[]{:S(2)}) copy-start(bf16[2,512,4,136]{1,3,2,0:T(8,128)(2,1)} %fusion.34) | copy-start | bytes 3342340
  165.8 5.4 %copy-start.5 = (f32[4,153,128]{2,1,0:T(8,128)S(1)}, f32[4,153,128]{2,1,0:T(8,128)}, u32[]{:S(2)}) copy-start(f32[4,153,128]{2,1,0:T(8,128)} %get-tuple-element.5) | copy-start | bytes 940036
  167.6 18.0 %all-to-all-start.7 = ((bf16[1024,4,128]{2,1,0:T(4,128)(2,1)}), bf16[1024,4,128]{2,1,0:T(4,128)(2,1)S(1)}, u32[]{:S(2)}, u32[]{:S(2)}) async-start(bf16[1024,4,128]{2,1,0:T(4,128)(2,1)} %copy.181), calls=%async_computation.7 | async-start | bytes 2097152 | tf_op jit(solution)/shard_map/all_to_all | solution.py:147
  185.5 18.0 %all-to-all-start.3 = ((bf16[1024,4,128]{2,1,0:T(4,128)(2,1)}), bf16[1024,4,128]{2,1,0:T(4,128)(2,1)S(1)}, u32[]{:S(2)}, u32[]{:S(2)}) async-start(bf16[1024,4,128]{2,1,0:T(4,128)(2,1)} %copy.154), calls=%async_computation.3 | async-start | bytes 2097152 | tf_op jit(solution)/shard_map/all_to_all | solution.py:147
  (22 other events, 57.2 us)
Sparse Core Ops, SparseCore 0:
  78.4 34.9 all-gather.4
  127.4 31.7 all-gather.6
where the time goes:
time: 219 us; the launch traced here: 217 us
  local copies, waits for them, and re-layouts  58.2 us (27%)
  waiting for transfers between devices  46.3 us (21%)
  starting transfers between devices  36.8 us (17%)
  matrix products  36.7 us (17%)
  other arithmetic  24.9 us (11%)
  between operations  14.1 us (6%)
    all_to_all x2, waiting for transfers between devices, per_device(): lax.all_to_all(mixed, 'head', split_axis=0, concat_axis=1, tiled=True)  21.3 us
    all_to_all x6, starting transfers between devices, gathered(): lax.all_to_all(tok[:, :, g], 'head', split_axis=1, concat_axis=0, tiled=T...  21.2 us
    all_to_all x6, waiting for transfers between devices, gathered(): lax.all_to_all(tok[:, :, g], 'head', split_axis=1, concat_axis=0, tiled=T...  18 us
    dot_general x2, matrix products, attend(): jnp.einsum('nhrs,nshv->nrhv', kernel, value_blocks, preferred_element_typ...  11.1 us
    ppermute x2, starting transfers between devices, shifted(): return lax.ppermute(shard, axis, pairs)  8.49 us
    another operation x4, local copies, waits for them, and re-layouts, attend(): key_head.reshape(chunks, WINDOW, heads_here, KD)  7.11 us
    all_to_all x2, starting transfers between devices, per_device(): lax.all_to_all(mixed, 'head', split_axis=0, concat_axis=1, tiled=True)  7.03 us
    all_gather x2, waiting for transfers between devices, attend(): everything = lax.all_gather(span_state, 'ctx')  6.98 us
  transfers between devices with their start and end apart: 12, of which 7 were waited for; matrix products, arithmetic and copies ran while one was open for 47% of the time, Pallas kernels for 0%

commit v1 on v0

--- a/solution.py
+++ b/solution.py
@@ -132,7 +132,20 @@
     span_rows = local_tokens * peers
 
     def gathered(tok, g, width):
-        moved = lax.all_to_all(tok[:, :, g], "head", split_axis=1, concat_axis=0, tiled=True)
+        x = tok[:, :, g]
+        ways, here_2 = (lax.axis_size("head"), lax.axis_index("head"))
+        width_2 = x.shape[1] // ways
+        lengths = list(x.shape)
+        lengths[1] = width_2
+        height = lengths[0]
+        lengths[0] = height * ways
+        full = jnp.zeros(lengths, x.dtype)
+        for mask in range(ways):
+            part = lax.dynamic_slice_in_dim(x, (here_2 ^ mask) * width_2, width_2, axis=1)
+            if mask:
+                part = lax.ppermute(part, "head", [(d, d ^ mask) for d in range(ways)])
+            full = lax.dynamic_update_slice_in_dim(full, part, (here_2 ^ mask) * height, axis=0)
+        moved = full
         return moved.reshape(span_rows, group_heads, width)
 
     outs = []

time: 219 us -> 229 us (1.046)
  local copies, waits for them, and re-layouts: 58.2 us -> 83.7 us
  waiting for transfers between devices: 46.3 us -> 32.7 us
  starting transfers between devices: 36.8 us -> 29.4 us
  other arithmetic: 24.9 us -> 28.5 us
    all_to_all x6 -> x0, starting transfers between devices: 21.2 us -> none  [gathered(): lax.all_to_all(tok[:, :, g], 'head', split_axis=1, concat_axis=0, tiled=T...]
    all_to_all x6 -> x0, waiting for transfers between devices: 18 us -> none  [gathered(): lax.all_to_all(tok[:, :, g], 'head', split_axis=1, concat_axis=0, tiled=T...]
    ppermute x0 -> x18, waiting for transfers between devices: none -> 15.3 us  [gathered(): part = lax.ppermute(part, 'head', [(d, d ^ mask) for d in range(ways)])]
    ppermute x0 -> x18, starting transfers between devices: none -> 13.6 us  [gathered(): part = lax.ppermute(part, 'head', [(d, d ^ mask) for d in range(ways)])]
    dynamic_update_slice x0 -> x26, local copies, waits for them, and re-layouts: none -> 12.6 us  [gathered(): lax.dynamic_update_slice_in_dim(full, part, (here_2 ^ mask) * height, axi...]
    another operation x0 -> x10, local copies, waits for them, and re-layouts: none -> 10.9 us  [the longest x4 10.6 us: attend(): value_blocks = value_head.reshape(block_count, block_rows, heads_here, VD)]
    all_to_all x2, waiting for transfers between devices: 21.3 us -> 13.1 us  [per_device(): lax.all_to_all(mixed, 'head', split_axis=0, concat_axis=1, tiled=True)]
    add x2, local copies, waits for them, and re-layouts: 0.27 us -> 6.01 us  [attend(): linear = (intra + inter).reshape(span_rows, heads_here, VD)]
  transfers between devices with their start and end apart: 12 -> 24, of which waited for: 7 -> 7; matrix products, arithmetic and copies ran while one was open for 47% -> 54% of each run, Pallas kernels for 0% -> 0%
where the time goes in v1:
time: 229 us; the launch traced here: 227 us
  local copies, waits for them, and re-layouts  83.7 us (37%)
  matrix products  38.5 us (17%)
  waiting for transfers between devices  32.7 us (14%)
  starting transfers between devices  29.4 us (13%)
  other arithmetic  28.5 us (12%)
  between operations  14.3 us (6%)
    ppermute x18, waiting for transfers between devices, gathered(): part = lax.ppermute(part, 'head', [(d, d ^ mask) for d in range(ways)])  15.3 us
    ppermute x18, starting transfers between devices, gathered(): part = lax.ppermute(part, 'head', [(d, d ^ mask) for d in range(ways)])  13.6 us
    all_to_all x2, waiting for transfers between devices, per_device(): lax.all_to_all(mixed, 'head', split_axis=0, concat_axis=1, tiled=True)  13.1 us
    dot_general x2, matrix products, attend(): jnp.einsum('nhrs,nshv->nrhv', kernel, value_blocks, preferred_element_typ...  12.8 us
    dynamic_update_slice x26, local copies, waits for them, and re-layouts, gathered(): lax.dynamic_update_slice_in_dim(full, part, (here_2 ^ mask) * height, axi...  12.6 us
    another operation x4, local copies, waits for them, and re-layouts, attend(): value_blocks = value_head.reshape(block_count, block_rows, heads_here, VD)  10.6 us
    all_to_all x2, starting transfers between devices, per_device(): lax.all_to_all(mixed, 'head', split_axis=0, concat_axis=1, tiled=True)  8 us
    ppermute x2, starting transfers between devices, shifted(): return lax.ppermute(shard, axis, pairs)  7.64 us
  transfers between devices with their start and end apart: 24, of which 7 were waited for; matrix products, arithmetic and copies ran while one was open for 54% of the time, Pallas kernels for 0%

profile of v1, /device:TPU:0, one launch (start us, length us, event | category | flops | bytes accessed | tf_op | source)
XLA Modules:
  0.0 227.1 jit_solution(12115467149981645781)
XLA Ops:
  11.4 3.3 %copy.165 = bf16[256,4096]{0,1:T(8,128)(2,1)S(1)} copy(bf16[256,4096]{1,0:T(8,128)(2,1)} %param.16) | data formatting | bytes 4194304 | tf_op jit(solution)/shard_map/reshape | solution.py:129
  31.1 3.2 %collective-permute-done.8 = bf16[256,1,4,16]{0,3,2,1:T(8,128)(2,1)S(1)} collective-permute-done((bf16[256,1,4,16]{0,3,2,1:T(8,128)(2,1)}, bf16[256,1,4,16]{0,3,2,1:T(8,128)(2,1)S(1)}, u32[]{:S(2)}, u32[]{:S(2)}) %collective-permute-start.8) | collective-permute-done | bytes 32800 | tf_op jit(solution)/shard_map/ppermute | solution.py:146
  49.4 6.0 %collective-permute-done.4 = bf16[256,1,4,16]{0,3,2,1:T(8,128)(2,1)S(1)} collective-permute-done((bf16[256,1,4,16]{0,3,2,1:T(8,128)(2,1)S(1)}, bf16[256,1,4,16]{0,3,2,1:T(8,128)(2,1)S(1)}, u32[]{:S(2)}, u32[]{:S(2)}) %collective-permute-start.4) | collective-permute-done | bytes 32800 | tf_op jit(solution)/shard_map/ppermute | solution.py:146
  55.6 3.3 %collective-permute-done.5 = bf16[256,1,4,16]{0,3,2,1:T(8,128)(2,1)S(1)} collective-permute-done((bf16[256,1,4,16]{0,3,2,1:T(8,128)(2,1)S(1)}, bf16[256,1,4,16]{0,3,2,1:T(8,128)(2,1)S(1)}, u32[]{:S(2)}, u32[]{:S(2)}) %collective-permute-start.5) | collective-permute-done | bytes 32800 | tf_op jit(solution)/shard_map/ppermute | solution.py:146
  67.4 2.6 %reshape.241 = bf16[2,512,4,153]{1,0,3,2:T(2,128)(2,1)} reshape(bf16[1024,4,153]{0,2,1:T(8,128)(2,1)} %get-tuple-element.33) | data formatting | bytes 2506752 | tf_op jit(solution)/shard_map/reshape | solution.py:46
  76.1 3.7 %copy.124 = bf16[2,512,4,128]{3,1,2,0:T(8,128)(2,1)} copy(bf16[2,512,4,128]{1,0,3,2:T(2,128)(2,1)} %reshape_reshape.38) | data formatting | bytes 2097152 | tf_op jit(solution)/shard_map/reshape;reshape | solution.py:66
  79.8 3.7 %fusion.113 = (f32[4,153,128]{2,1,0:T(8,128)}, f32[2,4,153,128]{3,2,1,0:T(8,128)}) fusion(bf16[2,512,4,128]{3,1,2,0:T(8,128)(2,1)} %copy.124, bf16[2,512,4,153]{1,0,3,2:T(2,128)(2,1)} %reshape.241), kind=kOutput, calls=%fused_computation.197 | convolution fusion | flops 160510464 | bytes 3241984 | tf_op jit(solution)/shard_map/nrhf,nrhv->nhfv/dot_general | solution.py:44
  107.0 4.1 %collective-permute-start.19 = (bf16[64,4,144]{0,2,1:T(8,128)(2,1)}, bf16[64,4,144]{0,2,1:T(8,128)(2,1)}, u32[]{:S(2)}, u32[]{:S(2)}) collective-permute-start(bf16[64,4,144]{0,2,1:T(8,128)(2,1)} %pad_maximum_fusion.7), channel_id=1, source_target_pairs={{0,4},{4,8},{8,12},{1,5},{5,9},{9,13},{2,6},{6,10},{10,14},{3,7},{... | collective-permute-start | bytes 221192 | tf_op jit(solution)/shard_map/ppermute | solution.py:19
  111.1 3.7 %copy.144 = bf16[2,512,4,128]{3,1,2,0:T(8,128)(2,1)} copy(bf16[2,512,4,128]{1,0,3,2:T(2,128)(2,1)} %reshape_reshape.44) | data formatting | bytes 2097152 | tf_op jit(solution)/shard_map/reshape;reshape | solution.py:66
  114.8 2.8 %fusion.114 = (f32[4,153,128]{2,1,0:T(8,128)}, f32[2,4,153,128]{3,2,1,0:T(8,128)S(1)}) fusion(bf16[2,512,4,128]{3,1,2,0:T(8,128)(2,1)} %copy.144, bf16[2,512,4,153]{1,0,3,2:T(2,128)(2,1)} %reshape.248), kind=kOutput, calls=%fused_computation.198 | convolution fusion | flops 160510464 | bytes 3241984 | tf_op jit(solution)/shard_map/nrhf,nrhv->nhfv/dot_general | solution.py:44
  121.3 3.5 %collective-permute-start.9 = (bf16[64,4,144]{0,2,1:T(8,128)(2,1)}, bf16[64,4,144]{0,2,1:T(8,128)(2,1)}, u32[]{:S(2)}, u32[]{:S(2)}) collective-permute-start(bf16[64,4,144]{0,2,1:T(8,128)(2,1)} %pad_maximum_fusion.8), channel_id=1, source_target_pairs={{0,4},{4,8},{8,12},{1,5},{5,9},{9,13},{2,6},{6,10},{10,14},{3,7},{... | collective-permute-start | bytes 221192 | tf_op jit(solution)/shard_map/ppermute | solution.py:19
  139.1 2.8 %pad_maximum_fusion.5 = bf16[1024,4,128]{0,2,1:T(8,128)(2,1)} fusion(bf16[960,4,128]{0,2,1:T(8,128)(2,1)} %slice_bitcast_fusion.1, bf16[64,4,128]{0,2,1:T(8,128)(2,1)S(1)} %slice.126), kind=kLoop, calls=%fused_computation.67 | loop fusion | flops 2097152 | bytes 2097152 | tf_op jit(solution)/shard_map/concatenate | solution.py:85
  145.8 3.3 %fusion.119 = (f32[16,4,64]{2,1,0:T(4,128)S(1)}, f32[16,4,64,128]{3,2,1,0:T(8,128)S(1)}) fusion(f32[16,4,64,128]{3,2,1,0:T(8,128)S(1)} %fusion.60, pred[16,64,128]{2,1,0:T(8,128)(4,1)S(1)} %copy-done.33), kind=kOutput, calls=%fused_computation.199 | output fusion | flops 3145855 | bytes 4341760 | tf_op jit(solution)/shard_map/sub | solution.py:112
  152.2 4.3 %all-gather.7.cloned.1.call-done = f32[16,153,128]{2,1,0:T(8,128)} async-done(((f32[4,153,128]{2,1,0:T(8,128)}), f32[16,153,128]{2,1,0:T(8,128)}) %all-gather.7.cloned.1.call-update) | async-done | bytes 1253392 | tf_op jit(solution)/shard_map/all_gather | solution.py:51
  156.5 2.9 %select_reduce_fusion.3 = (f32[4,153,128]{2,1,0:T(8,128)}, f32[4,153,128]{2,1,0:T(8,128)S(1)}) fusion(f32[4,4,153,128]{3,2,1,0:T(8,128)} %bitcast.202, pred[4]{0:T(512)(128)(4,1)S(1)} %copy-done.45, f32[4,4,153,128]{3,2,1,0:T(8,128)} %bitcast.203), kind=kLoop, calls=%fused_computation.64 | loop fusion | flops 1096704 | bytes 3133444 | tf_op jit(solution)/shard_map/reduce_sum | solution.py:54
  159.4 3.0 %fusion.39 = f32[2,4,128,512]{3,2,1,0:T(8,128)} fusion(bf16[2,512,4,136]{1,3,2,0:T(8,128)(2,1)S(1)} %copy-done.1, bf16[2,512,4,16]{1,3,2,0:T(8,128)(2,1)S(1)} %copy-done.23, bf16[153]{0:T(256)(128)(2,1)S(1)} %pad.33.clone, f32[1,4,153,128]{3,2,1,0:T(8,128)} %slice.131, f32[4,153,128]{2,1,0:T(8,128)S(1)} %get-tuple-element.6), kind=kOutput, calls=%fused_computation.54 | convolution fusion | flops 164505600 | bytes 3969330 | tf_op jit(solution)/shard_map/nrhf,nhfv->nrhv/dot_general | solution.py:78
  162.4 6.6 %multiply_reduce_fusion = (f32[2,512,4]{1,2,0:T(4,128)S(1)}, f32[2,512,4,128]{1,3,2,0:T(8,128)}) fusion(f32[2,4,128,512]{3,2,1,0:T(8,128)} %fusion.39, bf16[2,512,4,128]{3,1,2,0:T(8,128)(2,1)} %copy.144, pred[512,512]{1,0:T(8,128)(4,1)} %iota_compare_fusion, bf16[2,512,4,16]{1,0,3,2:T(2,128)(2,1)} %reshape_reshape.46, bf16[2,512,4,16]{1,0,3,2:T(2,128)(2,1)S(1)} %copy-done.12), kind=kOutput, calls=%fused_computation.33 | convolution fusion | flops 620228608 | bytes 5783552 | tf_op jit(solution)/shard_map/nhrs,nshv->nrhv/dot_general | solution.py:76
  169.0 2.9 %copy.148 = f32[2,512,4,128]{3,1,0,2:T(8,128)} copy(f32[2,512,4,128]{1,3,2,0:T(8,128)} %get-tuple-element.42) | data formatting | bytes 4194304 | tf_op jit(solution)/shard_map/add | solution.py:79
  175.9 4.5 %all-to-all-start.1 = ((bf16[1024,4,128]{2,1,0:T(4,128)(2,1)}), bf16[1024,4,128]{2,1,0:T(4,128)(2,1)}, u32[]{:S(2)}, u32[]{:S(2)}) async-start(bf16[1024,4,128]{2,1,0:T(4,128)(2,1)} %copy.157), calls=%async_computation.1 | async-start | bytes 2097152 | tf_op jit(solution)/shard_map/all_to_all | solution.py:160
  182.5 6.2 %multiply_reduce_fusion.1 = (f32[2,512,4]{1,2,0:T(4,128)S(1)}, f32[2,512,4,128]{1,3,2,0:T(8,128)}) fusion(f32[2,4,128,512]{3,2,1,0:T(8,128)} %fusion.34, bf16[2,512,4,128]{3,1,2,0:T(8,128)(2,1)S(1)} %copy-done.4, pred[512,512]{1,0:T(8,128)(4,1)S(1)} %copy-done.31, bf16[2,512,4,16]{1,0,3,2:T(2,128)(2,1)S(1)} %copy-done.34, ...), kind=kOutput, calls=%fused_computation.39 | convolution fusion | flops 620228608 | bytes 5783552 | tf_op jit(solution)/shard_map/nhrs,nshv->nrhv/dot_general | solution.py:76
  188.6 3.1 %copy.128 = f32[2,512,4,128]{3,1,0,2:T(8,128)} copy(f32[2,512,4,128]{1,3,2,0:T(8,128)} %get-tuple-element.46) | data formatting | bytes 4194304 | tf_op jit(solution)/shard_map/add | solution.py:79
  195.5 3.5 %all-to-all-start = ((bf16[1024,4,128]{2,1,0:T(4,128)(2,1)}), bf16[1024,4,128]{2,1,0:T(4,128)(2,1)S(1)}, u32[]{:S(2)}, u32[]{:S(2)}) async-start(bf16[1024,4,128]{2,1,0:T(4,128)(2,1)} %copy.137), calls=%async_computation | async-start | bytes 2097152 | tf_op jit(solution)/shard_map/all_to_all | solution.py:160
  200.4 13.1 %all-to-all-done = bf16[1024,4,128]{2,1,0:T(4,128)(2,1)S(1)} async-done(((bf16[1024,4,128]{2,1,0:T(4,128)(2,1)}), bf16[1024,4,128]{2,1,0:T(4,128)(2,1)S(1)}, u32[]{:S(2)}, u32[]{:S(2)}) %all-to-all-start) | async-done | bytes 1048608 | tf_op jit(solution)/shard_map/all_to_all | solution.py:160
  216.2 4.1 %copy.160 = bf16[256,4096]{1,0:T(8,128)(2,1)} copy(bf16[256,4096]{0,1:T(8,128)(2,1)} %bitcast.197) | data formatting | bytes 4194304 | tf_op jit(solution)/shard_map/reshape | solution.py:163
  (251 shorter events, 112.6 us)
Async XLA Ops:
  6.5 145.6 %all-gather.5.cloned.1.call-start = ((), (), s32[]{:S(2)}) async-start(), calls=%async_computation.2 | async-start | bytes 1638400 | tf_op jit(solution)/shard_map/all_gather | solution.py:51
  8.3 28.8 %collective-permute-start.16 = (bf16[256,1,4,16]{0,3,2,1:T(8,128)(2,1)}, bf16[256,1,4,16]{0,3,2,1:T(8,128)(2,1)}, u32[]{:S(2)}, u32[]{:S(2)}) collective-permute-start(bf16[256,1,4,16]{0,3,2,1:T(8,128)(2,1)} %get-tuple-element.30), channel_id=1, source_target_pairs={{0,1},{1,0},{2,3},{3,2},{4,5},{5,4},{6,7},{7,6},{8,9},{9,8},{10,11... | collective-permute-start | bytes 98312 | tf_op jit(solution)/shard_map/ppermute | solution.py:146
  8.8 29.1 %collective-permute-start.17 = (bf16[256,1,4,16]{0,3,2,1:T(8,128)(2,1)}, bf16[256,1,4,16]{0,3,2,1:T(8,128)(2,1)}, u32[]{:S(2)}, u32[]{:S(2)}) collective-permute-start(bf16[256,1,4,16]{0,3,2,1:T(8,128)(2,1)} %get-tuple-element.29), channel_id=1, source_target_pairs={{0,2},{1,3},{2,0},{3,1},{4,6},{5,7},{6,4},{7,5},{8,10},{9,11},{10,... | collective-permute-start | bytes 98312 | tf_op jit(solution)/shard_map/ppermute | solution.py:146
  11.3 27.9 %collective-permute-start.18 = (bf16[256,1,4,16]{0,3,2,1:T(8,128)(2,1)}, bf16[256,1,4,16]{0,3,2,1:T(8,128)(2,1)}, u32[]{:S(2)}, u32[]{:S(2)}) collective-permute-start(bf16[256,1,4,16]{0,3,2,1:T(8,128)(2,1)} %get-tuple-element.28), channel_id=1, source_target_pairs={{0,3},{1,2},{2,1},{3,0},{4,7},{5,6},{6,5},{7,4},{8,11},{9,10},{10,... | collective-permute-start | bytes 98312 | tf_op jit(solution)/shard_map/ppermute | solution.py:146
  16.8 82.2 %collective-permute-start.10 = (bf16[256,1,4,128]{0,3,2,1:T(8,128)(2,1)}, bf16[256,1,4,128]{0,3,2,1:T(8,128)(2,1)}, u32[]{:S(2)}, u32[]{:S(2)}) collective-permute-start(bf16[256,1,4,128]{0,3,2,1:T(8,128)(2,1)} %get-tuple-element.14), channel_id=1, source_target_pairs={{0,1},{1,0},{2,3},{3,2},{4,5},{5,4},{6,7},{7,6},{8,9},{9,8},{10,11... | collective-permute-start | bytes 786440 | tf_op jit(solution)/shard_map/ppermute | solution.py:146
  17.5 9.0 %collective-permute-start.6 = (bf16[256,1,4,16]{0,3,2,1:T(8,128)(2,1)}, bf16[256,1,4,16]{0,3,2,1:T(8,128)(2,1)}, u32[]{:S(2)}, u32[]{:S(2)}) collective-permute-start(bf16[256,1,4,16]{0,3,2,1:T(8,128)(2,1)} %get-tuple-element.24), channel_id=1, source_target_pairs={{0,1},{1,0},{2,3},{3,2},{4,5},{5,4},{6,7},{7,6},{8,9},{9,8},{10,11... | collective-permute-start | bytes 98312 | tf_op jit(solution)/shard_map/ppermute | solution.py:146
  26.5 4.1 %collective-permute-start.7 = (bf16[256,1,4,16]{0,3,2,1:T(8,128)(2,1)}, bf16[256,1,4,16]{0,3,2,1:T(8,128)(2,1)S(1)}, u32[]{:S(2)}, u32[]{:S(2)}) collective-permute-start(bf16[256,1,4,16]{0,3,2,1:T(8,128)(2,1)} %get-tuple-element.23), channel_id=1, source_target_pairs={{0,2},{1,3},{2,0},{3,1},{4,6},{5,7},{6,4},{7,5},{8,10},{9,11},{10,... | collective-permute-start | bytes 98312 | tf_op jit(solution)/shard_map/ppermute | solution.py:146
  30.6 3.6 %collective-permute-start.8 = (bf16[256,1,4,16]{0,3,2,1:T(8,128)(2,1)}, bf16[256,1,4,16]{0,3,2,1:T(8,128)(2,1)S(1)}, u32[]{:S(2)}, u32[]{:S(2)}) collective-permute-start(bf16[256,1,4,16]{0,3,2,1:T(8,128)(2,1)} %get-tuple-element.22), channel_id=1, source_target_pairs={{0,3},{1,2},{2,1},{3,0},{4,7},{5,6},{6,5},{7,4},{8,11},{9,10},{10,... | collective-permute-start | bytes 98312 | tf_op jit(solution)/shard_map/ppermute | solution.py:146
  34.3 65.7 %collective-permute-start.11 = (bf16[256,1,4,128]{0,3,2,1:T(8,128)(2,1)}, bf16[256,1,4,128]{0,3,2,1:T(8,128)(2,1)}, u32[]{:S(2)}, u32[]{:S(2)}) collective-permute-start(bf16[256,1,4,128]{0,3,2,1:T(8,128)(2,1)} %get-tuple-element.13), channel_id=1, source_target_pairs={{0,2},{1,3},{2,0},{3,1},{4,6},{5,7},{6,4},{7,5},{8,10},{9,11},{10,... | collective-permute-start | bytes 786440 | tf_op jit(solution)/shard_map/ppermute | solution.py:146
  37.1 8.6 %collective-permute-start.13 = (bf16[256,1,4,16]{0,3,2,1:T(8,128)(2,1)S(1)}, bf16[256,1,4,16]{0,3,2,1:T(8,128)(2,1)S(1)}, u32[]{:S(2)}, u32[]{:S(2)}) collective-permute-start(bf16[256,1,4,16]{0,3,2,1:T(8,128)(2,1)S(1)} %copy-done.41), channel_id=1, source_target_pairs={{0,1},{1,0},{2,3},{3,2},{4,5},{5,4},{6,7},{7,6},{8,9},{9,8},{10,11... | collective-permute-start | bytes 98312 | tf_op jit(solution)/shard_map/ppermute | solution.py:146
  37.9 8.1 %collective-permute-start.14 = (bf16[256,1,4,16]{0,3,2,1:T(8,128)(2,1)S(1)}, bf16[256,1,4,16]{0,3,2,1:T(8,128)(2,1)S(1)}, u32[]{:S(2)}, u32[]{:S(2)}) collective-permute-start(bf16[256,1,4,16]{0,3,2,1:T(8,128)(2,1)S(1)} %copy-done.40), channel_id=1, source_target_pairs={{0,2},{1,3},{2,0},{3,1},{4,6},{5,7},{6,4},{7,5},{8,10},{9,11},{10,... | collective-permute-start | bytes 98312 | tf_op jit(solution)/shard_map/ppermute | solution.py:146
  39.1 7.4 %collective-permute-start.15 = (bf16[256,1,4,16]{0,3,2,1:T(8,128)(2,1)S(1)}, bf16[256,1,4,16]{0,3,2,1:T(8,128)(2,1)S(1)}, u32[]{:S(2)}, u32[]{:S(2)}) collective-permute-start(bf16[256,1,4,16]{0,3,2,1:T(8,128)(2,1)S(1)} %copy-done.39), channel_id=1, source_target_pairs={{0,3},{1,2},{2,1},{3,0},{4,7},{5,6},{6,5},{7,4},{8,11},{9,10},{10,... | collective-permute-start | bytes 98312 | tf_op jit(solution)/shard_map/ppermute | solution.py:146
  45.7 24.3 %collective-permute-start = (bf16[256,1,4,128]{0,3,2,1:T(8,128)(2,1)}, bf16[256,1,4,128]{0,3,2,1:T(8,128)(2,1)}, u32[]{:S(2)}, u32[]{:S(2)}) collective-permute-start(bf16[256,1,4,128]{0,3,2,1:T(8,128)(2,1)} %get-tuple-element.11), channel_id=1, source_target_pairs={{0,1},{1,0},{2,3},{3,2},{4,5},{5,4},{6,7},{7,6},{8,9},{9,8},{10,11... | collective-permute-start | bytes 786440 | tf_op jit(solution)/shard_map/ppermute | solution.py:146
  46.0 26.5 %collective-permute-start.1 = (bf16[256,1,4,128]{0,3,2,1:T(8,128)(2,1)}, bf16[256,1,4,128]{0,3,2,1:T(8,128)(2,1)}, u32[]{:S(2)}, u32[]{:S(2)}) collective-permute-start(bf16[256,1,4,128]{0,3,2,1:T(8,128)(2,1)} %get-tuple-element.10), channel_id=1, source_target_pairs={{0,2},{1,3},{2,0},{3,1},{4,6},{5,7},{6,4},{7,5},{8,10},{9,11},{10,... | collective-permute-start | bytes 786440 | tf_op jit(solution)/shard_map/ppermute | solution.py:146
  46.5 1.3 collective-permute-start.3
  47.8 7.7 %collective-permute-start.4 = (bf16[256,1,4,16]{0,3,2,1:T(8,128)(2,1)S(1)}, bf16[256,1,4,16]{0,3,2,1:T(8,128)(2,1)S(1)}, u32[]{:S(2)}, u32[]{:S(2)}) collective-permute-start(bf16[256,1,4,16]{0,3,2,1:T(8,128)(2,1)S(1)} %get-tuple-element.20), channel_id=1, source_target_pairs={{0,2},{1,3},{2,0},{3,1},{4,6},{5,7},{6,4},{7,5},{8,10},{9,11},{10,... | collective-permute-start | bytes 98312 | tf_op jit(solution)/shard_map/ppermute | solution.py:146
  55.5 3.4 %collective-permute-start.5 = (bf16[256,1,4,16]{0,3,2,1:T(8,128)(2,1)S(1)}, bf16[256,1,4,16]{0,3,2,1:T(8,128)(2,1)S(1)}, u32[]{:S(2)}, u32[]{:S(2)}) collective-permute-start(bf16[256,1,4,16]{0,3,2,1:T(8,128)(2,1)S(1)} %get-tuple-element.19), channel_id=1, source_target_pairs={{0,3},{1,2},{2,1},{3,0},{4,7},{5,6},{6,5},{7,4},{8,11},{9,10},{10,... | collective-permute-start | bytes 98312 | tf_op jit(solution)/shard_map/ppermute | solution.py:146
  58.8 14.7 %collective-permute-start.2 = (bf16[256,1,4,128]{0,3,2,1:T(8,128)(2,1)}, bf16[256,1,4,128]{0,3,2,1:T(8,128)(2,1)}, u32[]{:S(2)}, u32[]{:S(2)}) collective-permute-start(bf16[256,1,4,128]{0,3,2,1:T(8,128)(2,1)} %get-tuple-element.9), channel_id=1, source_target_pairs={{0,3},{1,2},{2,1},{3,0},{4,7},{5,6},{6,5},{7,4},{8,11},{9,10},{10,... | collective-permute-start | bytes 786440 | tf_op jit(solution)/shard_map/ppermute | solution.py:146
  70.0 30.9 %collective-permute-start.12 = (bf16[256,1,4,128]{0,3,2,1:T(8,128)(2,1)}, bf16[256,1,4,128]{0,3,2,1:T(8,128)(2,1)}, u32[]{:S(2)}, u32[]{:S(2)}) collective-permute-start(bf16[256,1,4,128]{0,3,2,1:T(8,128)(2,1)} %get-tuple-element.12), channel_id=1, source_target_pairs={{0,3},{1,2},{2,1},{3,0},{4,7},{5,6},{6,5},{7,4},{8,11},{9,10},{10,... | collective-permute-start | bytes 786440 | tf_op jit(solution)/shard_map/ppermute | solution.py:146
  83.5 73.0 %all-gather.7.cloned.1.call-start = ((), (), s32[]{:S(2)}) async-start(), calls=%async_computation.3 | async-start | bytes 1638400 | tf_op jit(solution)/shard_map/all_gather | solution.py:51
  107.0 18.7 %collective-permute-start.19 = (bf16[64,4,144]{0,2,1:T(8,128)(2,1)}, bf16[64,4,144]{0,2,1:T(8,128)(2,1)}, u32[]{:S(2)}, u32[]{:S(2)}) collective-permute-start(bf16[64,4,144]{0,2,1:T(8,128)(2,1)} %pad_maximum_fusion.7), channel_id=1, source_target_pairs={{0,4},{4,8},{8,12},{1,5},{5,9},{9,13},{2,6},{6,10},{10,14},{3,7},{... | collective-permute-start | bytes 221192 | tf_op jit(solution)/shard_map/ppermute | solution.py:19
  121.3 13.4 %collective-permute-start.9 = (bf16[64,4,144]{0,2,1:T(8,128)(2,1)}, bf16[64,4,144]{0,2,1:T(8,128)(2,1)}, u32[]{:S(2)}, u32[]{:S(2)}) collective-permute-start(bf16[64,4,144]{0,2,1:T(8,128)(2,1)} %pad_maximum_fusion.8), channel_id=1, source_target_pairs={{0,4},{4,8},{8,12},{1,5},{5,9},{9,13},{2,6},{6,10},{10,14},{3,7},{... | collective-permute-start | bytes 221192 | tf_op jit(solution)/shard_map/ppermute | solution.py:19
  175.9 19.6 %all-to-all-start.1 = ((bf16[1024,4,128]{2,1,0:T(4,128)(2,1)}), bf16[1024,4,128]{2,1,0:T(4,128)(2,1)}, u32[]{:S(2)}, u32[]{:S(2)}) async-start(bf16[1024,4,128]{2,1,0:T(4,128)(2,1)} %copy.157), calls=%async_computation.1 | async-start | bytes 2097152 | tf_op jit(solution)/shard_map/all_to_all | solution.py:160
  195.5 18.0 %all-to-all-start = ((bf16[1024,4,128]{2,1,0:T(4,128)(2,1)}), bf16[1024,4,128]{2,1,0:T(4,128)(2,1)S(1)}, u32[]{:S(2)}, u32[]{:S(2)}) async-start(bf16[1024,4,128]{2,1,0:T(4,128)(2,1)} %copy.137), calls=%async_computation | async-start | bytes 2097152 | tf_op jit(solution)/shard_map/all_to_all | solution.py:160
  (46 other events, 219.9 us)
Sparse Core Ops, SparseCore 0:
  83.6 33.3 all-gather.4
  125.7 30.6 all-gather.6
